TPU v7x, 128 devices: a whole 4x4x4 slice. The times are simulated.
128 devices in a mesh: pipe: 32 (over x, z, y_hi), dp: 4 (over y_lo, core).
Axes of the slice: x: 4, y: 4 (y_hi: 2, y_lo: 2; y = y_hi * 2 + y_lo), z: 4, core: 2. Of those that a mesh axis runs over, the one named last changes fastest.
Arguments:
- parked: bfloat16 [32, 8, 128, 8192], P('pipe', 'dp'), may hold values from -160 to 160
- slot_order: int32 [32, 4, 2], P('pipe', 'dp'), may hold values from 0 to 1, each once within a row
- segment_ids: int32 [32, 8, 128], P('pipe', 'dp'), may hold values from 0 to 3, never falling along the last dimension, each value on 1 to 64 neighbouring positions
- queries: bfloat16 [32, 8, 128, 4096], P('pipe', 'dp'), may hold values from -17 to 17
- out_grad: bfloat16 [32, 8, 128, 4096], P('pipe', 'dp'), may hold values from -4 to 4
- norm_gain: bfloat16 [32, 8192], P('pipe'), may hold values from 0.5 to 1.5
- kv_weight: bfloat16 [32, 8192, 1024], P('pipe', 'dp'), may hold values from -0.0625 to 0.0625
Outputs:
- upstream_grad: bfloat16 [32, 8, 128, 8192], P('pipe', 'dp')
- kv_weight_grad: bfloat16 [32, 8192, 1024], P('pipe', 'dp')
- gain_grad: float32 [32, 8192], P('pipe')
All inputs are finite; a program needn't handle non-finite values.
Results may differ from a plain program's by a relative error of at most 0.012.
The roundings to bfloat16 on the way count: a program that leaves them out, or rounds other values in their place, can miss the bound.
Values may be sent and summed in bfloat16 or wider, within the bound.
No kernel may reach another device: no remote copies, remote signals or barrier semaphores. Data moves between devices by JAX's collectives and lax.ppermute only.
A program may use at most 128 MiB of HBM per device.

v0:
```python
import math

import jax
import jax.numpy as jnp
from jax import lax
from jax.sharding import PartitionSpec as P

QH = 32
KVH = 4
HD = 128


EPSILON = 1e-05


def shifted(value, axis, steps):
    count = lax.axis_size(axis)
    leading, last = (max(0, -steps), min(count, count - steps))
    return lax.ppermute(value, axis, [(source, source + steps) for source in range(leading, last)])


def attention_grads(queries, out_grad, keys, values, segments):
    batch_count = queries.shape[0]
    seq_len = queries.shape[1]
    group_size = QH // KVH
    scaling = 1.0 / math.sqrt(HD)
    query_heads = queries.reshape(batch_count, seq_len, KVH, group_size, HD)
    grad_heads = out_grad.reshape(batch_count, seq_len, KVH, group_size, HD)
    key_heads = keys.reshape(batch_count, seq_len, KVH, HD)
    value_heads = values.reshape(batch_count, seq_len, KVH, HD)
    scores = (
        jnp.einsum("bqhgd,bkhd->bhgqk", query_heads, key_heads, preferred_element_type=jnp.float32)
        * scaling
    )
    position = jnp.arange(seq_len)
    causal = position[None, :] <= position[:, None]
    allowed = causal[None] & (segments[:, :, None] == segments[:, None, :])
    scores = jnp.where(allowed[:, None, None], scores, -1e30)
    highest = jnp.max(scores, axis=-1, keepdims=True)
    weights = jnp.exp(scores - highest)
    probabilities = weights / jnp.sum(weights, axis=-1, keepdims=True)
    probs_low = probabilities.astype(jnp.bfloat16)
    value_grad = jnp.einsum(
        "bhgqk,bqhgd->bkhd", probs_low, grad_heads, preferred_element_type=jnp.float32
    )
    prob_grad = jnp.einsum(
        "bqhgd,bkhd->bhgqk", grad_heads, value_heads, preferred_element_type=jnp.float32
    )
    row_dot = jnp.sum(probabilities * prob_grad, axis=-1, keepdims=True)
    score_grad = (probabilities * (prob_grad - row_dot) * scaling).astype(jnp.bfloat16)
    key_grad = jnp.einsum(
        "bhgqk,bqhgd->bkhd", score_grad, query_heads, preferred_element_type=jnp.float32
    )
    key_low = key_grad.astype(jnp.bfloat16).reshape(batch_count, seq_len, KVH * HD)
    value_low = value_grad.astype(jnp.bfloat16).reshape(batch_count, seq_len, KVH * HD)
    return jnp.concatenate([key_low, value_low], axis=-1)


def local(parked, slot_order, segment_ids, queries, out_grad, norm_gain, kv_weight):
    sections = lax.axis_size("pipe")
    stored = parked[0]
    micro_count, seq_len, feature_count = stored.shape
    token_count = micro_count * seq_len
    flat_stored = stored.reshape(token_count, feature_count)
    spread = lax.all_to_all(flat_stored, "pipe", split_axis=1, concat_axis=0, tiled=True)
    blocks = spread.reshape(sections, token_count, feature_count // sections)[::-1]
    fetched = lax.all_to_all(blocks, "pipe", split_axis=0, concat_axis=2, tiled=True).reshape(
        micro_count, seq_len, feature_count
    )
    inputs = jnp.take(fetched, slot_order[0, 0], axis=0)
    flat_inputs = inputs.reshape(token_count, feature_count)
    inputs_wide = flat_inputs.astype(jnp.float32)
    inverse = lax.rsqrt(jnp.mean(inputs_wide * inputs_wide, axis=-1) + EPSILON)
    gain_full = norm_gain[0].astype(jnp.float32)
    local_weight = kv_weight[0]
    slice_width = local_weight.shape[0]
    start_col = lax.axis_index("dp") * slice_width
    gain_local = lax.dynamic_slice_in_dim(gain_full, start_col, slice_width)
    columns = lax.all_to_all(flat_inputs, "dp", split_axis=1, concat_axis=0, tiled=True)
    scales = lax.all_gather(inverse, "dp", axis=0, tiled=True)
    columns_wide = columns.astype(jnp.float32)
    normed_cols = (columns_wide * scales[:, None] * gain_local).astype(jnp.bfloat16)
    normed = (inputs_wide * inverse[:, None] * gain_full).astype(jnp.bfloat16)
    full_weight = lax.all_gather(local_weight, "dp", axis=0, tiled=True)
    projected = jnp.dot(normed, full_weight, preferred_element_type=jnp.float32)
    projected_low = projected.astype(jnp.bfloat16).reshape(micro_count, seq_len, -1)
    head_span = projected_low.shape[-1] // 2
    kv_grads = attention_grads(
        queries[0],
        out_grad[0],
        projected_low[..., :head_span],
        projected_low[..., head_span:],
        segment_ids[0],
    )
    kv_grads = kv_grads.reshape(token_count, -1)
    all_kv_grads = lax.all_gather(kv_grads, "dp", axis=0, tiled=True)
    weight_grad = lax.dot_general(
        normed_cols, all_kv_grads, (((0,), (0,)), ((), ())), preferred_element_type=jnp.float32
    ).astype(jnp.bfloat16)
    normed_grad = lax.dot_general(
        kv_grads, full_weight, (((1,), (1,)), ((), ())), preferred_element_type=jnp.float32
    )
    scaled_grad = normed_grad * gain_full
    inner_mean = jnp.mean(scaled_grad * inputs_wide, axis=-1)
    scale_col = inverse[:, None]
    input_grad = (
        scale_col * scaled_grad - inputs_wide * scale_col**3 * inner_mean[:, None]
    ).astype(jnp.bfloat16)
    gain_term = jnp.sum(normed_grad * inputs_wide * scale_col, axis=0)
    gain_grad = lax.psum(gain_term, "dp")
    upstream = shifted(input_grad.reshape(micro_count, seq_len, feature_count), "pipe", -1)
    return (upstream[None], weight_grad[None], gain_grad[None])


def solution(mesh):
    return jax.shard_map(
        local,
        mesh=mesh,
        in_specs=(
            P("pipe", "dp", None, None),
            P("pipe", "dp", None),
            P("pipe", "dp", None),
            P("pipe", "dp", None, None),
            P("pipe", "dp", None, None),
            P("pipe", None),
            P("pipe", "dp", None),
        ),
        out_specs=(P("pipe", "dp", None, None), P("pipe", "dp", None), P("pipe", None)),
        check_vma=False,
    )
```

profile of v0, /device:TPU:66, one launch (start us, length us, event | category | flops | bytes accessed | tf_op | source)
XLA Modules:
  0.0 496.7 jit_solution(14236564483229686694)
XLA Ops:
  13.9 69.4 %all_to_all.41 = bf16[256,32,256]{2,0,1:T(8,128)(2,1)} all-to-all(bf16[256,32,256]{2,0,1:T(8,128)(2,1)S(1)} %copy.46), channel_id=1, replica_groups=mesh['pipe'=32,'dp'=4] {'pipe'}, dimensions={1} | all-to-all | bytes 8388608 | tf_op jit(solution)/shard_map/all_to_all | solution.py:65
  83.3 4.7 rev.3
  88.0 8.6 %all-to-all-start.1 = ((bf16[32,256,256]{2,1,0:T(8,128)(2,1)}), bf16[32,256,256]{2,1,0:T(8,128)(2,1)}, u32[]{:S(2)}, u32[]{:S(2)}) async-start(bf16[32,256,256]{2,1,0:T(8,128)(2,1)} %rev.3), calls=%async_computation.1 | async-start | bytes 8388608 | tf_op jit(solution)/shard_map/all_to_all | solution.py:67
  101.0 55.9 %all-to-all-done.1 = bf16[32,256,256]{2,1,0:T(8,128)(2,1)} async-done(((bf16[32,256,256]{2,1,0:T(8,128)(2,1)}), bf16[32,256,256]{2,1,0:T(8,128)(2,1)}, u32[]{:S(2)}, u32[]{:S(2)}) %all-to-all-start.1) | async-done | bytes 4194336 | tf_op jit(solution)/shard_map/all_to_all | solution.py:67
  156.9 6.6 %copy.47 = bf16[1,256,32,256]{3,2,1,0:T(8,128)(2,1)} copy(bf16[1,256,32,256]{3,1,2,0:T(8,128)(2,1)} %bitcast.3) | data formatting | bytes 8388608 | tf_op jit(solution)/shard_map/all_to_all | solution.py:67
  163.5 7.4 %reshape.137 = bf16[2,128,8192]{2,1,0:T(8,128)(2,1)} reshape(bf16[1,256,32,256]{3,2,1,0:T(8,128)(2,1)} %copy.47) | data formatting | bytes 8388608 | tf_op jit(solution)/shard_map/reshape | solution.py:67
  170.8 5.0 fusion.71
  175.8 3.6 gather_fusion
  187.8 7.8 %gather.10 = bf16[256,4,2048]{2,1,0:T(4,128)(2,1)} reshape(bf16[2,128,8192]{2,1,0:T(8,128)(2,1)} %constant_dynamic-update-slice_fusion) | data formatting | bytes 8388608 | tf_op jit(solution)/shard_map/jit(_take)/gather | solution.py:70
  195.6 4.3 broadcast_select_fusion
  199.8 4.3 copy.58
  204.1 4.8 all-to-all-start.2
  213.0 4.7 bitcast_select_fusion.1
  217.7 76.3 %all-gather.7.cloned.1.call-done = bf16[1,8192,1024]{2,1,0:T(8,128)(2,1)} async-done(((bf16[1,2048,1024]{2,1,0:T(8,128)(2,1)}), bf16[1,8192,1024]{2,1,0:T(8,128)(2,1)}) %all-gather.7.cloned.1.call-update) | async-done | bytes 16777232 | tf_op jit(solution)/shard_map/all_gather | solution.py:84
  294.0 11.6 %fusion.36 = bf16[256,1024]{1,0:T(8,128)(2,1)S(1)} fusion(bf16[1,8192,1024]{2,1,0:T(8,128)(2,1)} %all-gather.7.cloned.1.call-done, bf16[256,8192]{1,0:T(8,128)(2,1)} %bitcast_select_fusion.1, f32[8192]{0:T(1024)S(1)} %bitcast.156, f32[256]{0:T(256)S(1)} %get-tuple-element.10), kind=kOutput, calls=%fused_computation.51 | convolution fusion | flops 4303618048 | bytes 21529600 | tf_op jit(solution)/shard_map/dot_general | solution.py:85
  312.5 7.5 %fusion.62 = bf16[2,128,4,128]{3,1,2,0:T(8,128)(2,1)S(1)} fusion(bf16[2,128,4,8,128]{4,3,2,1,0:T(8,128)(2,1)S(1)} %bitcast.145, f32[2,4,128,128,8]{3,2,4,1,0:T(8,128)} %fusion.31, f32[2,4,8,128,128]{3,4,2,1,0:T(8,128)} %copy-done.7, f32[2,4,8,128]{3,2,1,0:T(8,128)S(1)} %get-tuple-element.11), kind=kOutput, calls=%fused_computation.57 | convolution fusion | flops 275914880 | bytes 10780672 | tf_op jit(solution)/shard_map/bhgqk,bqhgd->bkhd/dot_general | solution.py:51
  320.6 10.4 %fusion.13 = (f32[8192]{0:T(1024)S(1)}, f32[256]{0:T(256)S(1)}, f32[256,8192]{1,0:T(8,128)S(1)}) fusion(bf16[256,8192]{1,0:T(8,128)(2,1)} %bitcast_select_fusion.1, f32[256]{0:T(256)S(1)} %get-tuple-element.10, f32[8192]{0:T(1024)S(1)} %bitcast.157, bf16[256,1024]{1,0:T(8,128)(2,1)S(1)} %bitcast_dynamic-update-slice_fusion, ...), kind=kOutput, calls=%fused_computation.19 | convolution fusion | flops 4309639168 | bytes 29952000 | tf_op jit(solution)/shard_map/dot_general | solution.py:100
  331.0 6.2 %fusion.10 = bf16[256,8192]{1,0:T(8,128)(2,1)} fusion(f32[256,8192]{1,0:T(8,128)S(1)} %get-tuple-element.13, f32[256]{0:T(256)S(1)} %broadcast_multiply_fusion, f32[256]{0:T(256)S(1)} %multiply_multiply_fusion, f32[8192]{0:T(1024)S(1)} %bitcast.158, f32[256]{0:T(256)S(1)} %get-tuple-element.10, bf16[2,128,8192]{2,1,0:T(8,128)(2,1)} %constant_dynamic-update-slice_fusion, ...), kind=kLoop, calls=%fused_computation.16 | loop fusion | flops 16777216 | bytes 16813312 | tf_op jit(solution)/shard_map/convert_element_type | solution.py:108
  337.1 11.4 %collective-permute-start = (bf16[2,128,8192]{2,1,0:T(8,128)(2,1)}, bf16[2,128,8192]{2,1,0:T(8,128)(2,1)}, u32[]{:S(2)}, u32[]{:S(2)}) collective-permute-start(bf16[2,128,8192]{2,1,0:T(8,128)(2,1)} %bitcast.25), channel_id=1, source_target_pairs={{4,0},{8,4},{12,8},{16,12},{20,16},{24,20},{28,24},{32,28},{36,32}... | collective-permute-start | bytes 12582920 | tf_op jit(solution)/shard_map/ppermute | solution.py:19
  348.6 107.6 %all-gather.1 = f32[4,1,256]{2,1,0:T(1,128)S(1)} all-gather(f32[1,1,256]{2,1,0:T(1,128)S(1)} %bitcast.163), channel_id=1, replica_groups=mesh['pipe'=32,'dp'=4] {'dp'}, dimensions={0}, use_global_device_ids=true | all-gather | bytes 5120 | tf_op jit(solution)/shard_map/all_gather | solution.py:80
  456.2 5.2 %fusion.15 = bf16[1024,2048]{1,0:T(8,128)(2,1)} fusion(f32[2048]{0:T(1024)S(1)} %bitcast.159, f32[1024]{0:T(1024)S(1)} %bitcast.161, bf16[256,4,2048]{2,0,1:T(8,128)(2,1)} %all-to-all-done.2), kind=kLoop, calls=%fused_computation.22 | loop fusion | flops 8388608 | bytes 8400896 | tf_op jit(solution)/shard_map/convert_element_type | solution.py:82
  461.3 14.2 %psum.7 = f32[1,8192]{1,0:T(1,128)} all-reduce(f32[1,8192]{1,0:T(1,128)S(1)} %bitcast.160), channel_id=1, replica_groups=mesh['pipe'=32,'dp'=4] {'dp'}, use_global_device_ids=true, to_apply=%region_6.7 | all-reduce | flops 8192 | bytes 65536 | tf_op jit(solution)/shard_map/psum | solution.py:110
  475.5 9.5 %convert_bitcast_fusion = bf16[1,2048,1024]{2,1,0:T(8,128)(2,1)} fusion(bf16[1024,2048]{1,0:T(8,128)(2,1)} %fusion.15, bf16[1024,1024]{1,0:T(8,128)(2,1)} %all-gather.5.cloned.1.call-done), kind=kOutput, calls=%fused_computation.31 | convolution fusion | flops 4297064448 | bytes 10485760 | tf_op jit(solution)/shard_map/dot_general | solution.py:97
  485.0 4.6 copy.99
  (53 shorter events, 30.8 us)
Async XLA Ops:
  7.2 286.9 %all-gather.7.cloned.1.call-start = ((), (), s32[]{:S(2)}) async-start(), calls=%async_computation.4 | async-start | bytes 20971520 | tf_op jit(solution)/shard_map/all_gather | solution.py:84
  88.0 8.6 %copy-start.4 = (bf16[1,8192]{1,0:T(2,128)(2,1)S(1)}, bf16[1,8192]{1,0:T(2,128)(2,1)}, u32[]{:S(2)}) copy-start(bf16[1,8192]{1,0:T(2,128)(2,1)} %param.12) | copy-start | bytes 49156
  88.0 68.9 %all-to-all-start.1 = ((bf16[32,256,256]{2,1,0:T(8,128)(2,1)}), bf16[32,256,256]{2,1,0:T(8,128)(2,1)}, u32[]{:S(2)}, u32[]{:S(2)}) async-start(bf16[32,256,256]{2,1,0:T(8,128)(2,1)} %rev.3), calls=%async_computation.1 | async-start | bytes 8388608 | tf_op jit(solution)/shard_map/all_to_all | solution.py:67
  96.6 2.3 copy-start.2
  96.7 4.1 copy-start.6
  96.7 4.2 copy-start.5
  183.0 3.3 copy-start.1
  204.1 252.1 %all-to-all-start.2 = ((bf16[256,4,2048]{2,0,1:T(8,128)(2,1)}), bf16[256,4,2048]{2,0,1:T(8,128)(2,1)}, u32[]{:S(2)}, u32[]{:S(2)}) async-start(bf16[256,4,2048]{2,0,1:T(8,128)(2,1)} %copy.58), calls=%async_computation.2 | async-start | bytes 8388608 | tf_op jit(solution)/shard_map/all_to_all | solution.py:79
  209.0 266.5 %all-gather.5.cloned.1.call-start = ((), (), s32[]{:S(2)}) async-start(), calls=%async_computation.3 | async-start | bytes 2621440 | tf_op jit(solution)/shard_map/all_gather | solution.py:96
  306.9 1.6 copy-start
  308.3 3.2 copy-start.7
  320.5 10.4 %copy-start.3 = (bf16[256,1024]{1,0:T(8,128)(2,1)}, bf16[256,1024]{1,0:T(8,128)(2,1)S(1)}, u32[]{:S(2)}) copy-start(bf16[256,1024]{1,0:T(8,128)(2,1)S(1)} %bitcast_dynamic-update-slice_fusion) | copy-start | bytes 1572868
  337.1 147.8 %collective-permute-start = (bf16[2,128,8192]{2,1,0:T(8,128)(2,1)}, bf16[2,128,8192]{2,1,0:T(8,128)(2,1)}, u32[]{:S(2)}, u32[]{:S(2)}) collective-permute-start(bf16[2,128,8192]{2,1,0:T(8,128)(2,1)} %bitcast.25), channel_id=1, source_target_pairs={{4,0},{8,4},{12,8},{16,12},{20,16},{24,20},{28,24},{32,28},{36,32}... | collective-permute-start | bytes 12582920 | tf_op jit(solution)/shard_map/ppermute | solution.py:19
Sparse Core Ops, SparseCore 0:
  9.6 284.3 all-gather.6
  348.7 43.3 all-gather.4
where the time goes:
time: 502 us; the launch traced here: 497 us
  blocking collectives  191 us (38%)
  waiting for transfers between devices  133 us (26%)
  local copies, waits for them, and re-layouts  63.5 us (13%)
  matrix products  43.8 us (9%)
  starting transfers between devices  25.5 us (5%)
  other arithmetic  25.2 us (5%)
  between operations  14.5 us (3%)
    all_gather x1, blocking collectives, local(): scales = lax.all_gather(inverse, 'dp', axis=0, tiled=True)  108 us
    all_gather x1, waiting for transfers between devices, local(): full_weight = lax.all_gather(local_weight, 'dp', axis=0, tiled=True)  76.3 us
    all_to_all x1, blocking collectives, local(): lax.all_to_all(flat_stored, 'pipe', split_axis=1, concat_axis=0, tiled=True)  69.4 us
    all_to_all x1, waiting for transfers between devices, local(): lax.all_to_all(blocks, 'pipe', split_axis=0, concat_axis=2, tiled=True)  55.9 us
    gather x4, local copies, waits for them, and re-layouts, local(): inputs = jnp.take(fetched, slot_order[0, 0], axis=0)  20 us
    unnamed x25, local copies, waits for them, and re-layouts  17.7 us
    psum x1, blocking collectives, local(): gain_grad = lax.psum(gain_term, 'dp')  14.2 us
    dot_general x1, matrix products, local(): projected = jnp.dot(normed, full_weight, preferred_element_type=jnp.float32)  11.6 us
  transfers between devices with their start and end apart: 5, of which 2 were waited for; matrix products, arithmetic and copies ran while one was open for 26% of the time, Pallas kernels for 0%

commit v1 on v0

--- a/solution.py
+++ b/solution.py
@@ -11,12 +11,6 @@
 
 
 EPSILON = 1e-05
-
-
-def shifted(value, axis, steps):
-    count = lax.axis_size(axis)
-    leading, last = (max(0, -steps), min(count, count - steps))
-    return lax.ppermute(value, axis, [(source, source + steps) for source in range(leading, last)])
 
 
 def attention_grads(queries, out_grad, keys, values, segments):
@@ -58,31 +52,46 @@
 
 def local(parked, slot_order, segment_ids, queries, out_grad, norm_gain, kv_weight):
     sections = lax.axis_size("pipe")
+    replicas = lax.axis_size("dp")
+    me = lax.axis_index("dp")
     stored = parked[0]
     micro_count, seq_len, feature_count = stored.shape
     token_count = micro_count * seq_len
+    width = feature_count // replicas
+    axes = ("pipe", "dp")
+
     flat_stored = stored.reshape(token_count, feature_count)
-    spread = lax.all_to_all(flat_stored, "pipe", split_axis=1, concat_axis=0, tiled=True)
-    blocks = spread.reshape(sections, token_count, feature_count // sections)[::-1]
-    fetched = lax.all_to_all(blocks, "pipe", split_axis=0, concat_axis=2, tiled=True).reshape(
-        micro_count, seq_len, feature_count
-    )
-    inputs = jnp.take(fetched, slot_order[0, 0], axis=0)
-    flat_inputs = inputs.reshape(token_count, feature_count)
-    inputs_wide = flat_inputs.astype(jnp.float32)
-    inverse = lax.rsqrt(jnp.mean(inputs_wide * inputs_wide, axis=-1) + EPSILON)
+    stored_wide = flat_stored.astype(jnp.float32)
+    inv_src = lax.rsqrt(jnp.mean(stored_wide * stored_wide, axis=-1) + EPSILON)
+
+    received = []
+    for k in range(replicas):
+        pairs = [
+            (s * replicas + d, (sections - 1 - s) * replicas + (d + k) % replicas)
+            for s in range(sections)
+            for d in range(replicas)
+        ]
+        col = (me + k) % replicas
+        block = lax.dynamic_slice_in_dim(flat_stored, col * width, width, axis=1)
+        received.append(lax.ppermute((block, inv_src), axes, pairs))
+
+    orders = lax.all_gather(slot_order[0, 0], "dp", axis=0, tiled=False)
+    replica_ids = jnp.arange(replicas, dtype=jnp.int32)
+    source_k = (me - replica_ids) % replicas
+    rows = (source_k[:, None] * micro_count + orders).reshape(-1)
+    blocks = jnp.stack([b for b, _ in received]).reshape(replicas * micro_count, seq_len, width)
+    invs = jnp.stack([v for _, v in received]).reshape(replicas * micro_count, seq_len)
+    x_cols = jnp.take(blocks, rows, axis=0).reshape(replicas * token_count, width)
+    inverse = jnp.take(invs, rows, axis=0).reshape(replicas * token_count)
+
     gain_full = norm_gain[0].astype(jnp.float32)
+    gain_local = lax.dynamic_slice_in_dim(gain_full, me * width, width)
+    x_wide = x_cols.astype(jnp.float32)
+    scale_col = inverse[:, None]
+    normed = (x_wide * scale_col * gain_local).astype(jnp.bfloat16)
     local_weight = kv_weight[0]
-    slice_width = local_weight.shape[0]
-    start_col = lax.axis_index("dp") * slice_width
-    gain_local = lax.dynamic_slice_in_dim(gain_full, start_col, slice_width)
-    columns = lax.all_to_all(flat_inputs, "dp", split_axis=1, concat_axis=0, tiled=True)
-    scales = lax.all_gather(inverse, "dp", axis=0, tiled=True)
-    columns_wide = columns.astype(jnp.float32)
-    normed_cols = (columns_wide * scales[:, None] * gain_local).astype(jnp.bfloat16)
-    normed = (inputs_wide * inverse[:, None] * gain_full).astype(jnp.bfloat16)
-    full_weight = lax.all_gather(local_weight, "dp", axis=0, tiled=True)
-    projected = jnp.dot(normed, full_weight, preferred_element_type=jnp.float32)
+    partial = jnp.dot(normed, local_weight, preferred_element_type=jnp.float32)
+    projected = lax.psum_scatter(partial, "dp", scatter_dimension=0, tiled=True)
     projected_low = projected.astype(jnp.bfloat16).reshape(micro_count, seq_len, -1)
     head_span = projected_low.shape[-1] // 2
     kv_grads = attention_grads(
@@ -95,20 +104,34 @@
     kv_grads = kv_grads.reshape(token_count, -1)
     all_kv_grads = lax.all_gather(kv_grads, "dp", axis=0, tiled=True)
     weight_grad = lax.dot_general(
-        normed_cols, all_kv_grads, (((0,), (0,)), ((), ())), preferred_element_type=jnp.float32
+        normed, all_kv_grads, (((0,), (0,)), ((), ())), preferred_element_type=jnp.float32
     ).astype(jnp.bfloat16)
     normed_grad = lax.dot_general(
-        kv_grads, full_weight, (((1,), (1,)), ((), ())), preferred_element_type=jnp.float32
+        all_kv_grads, local_weight, (((1,), (1,)), ((), ())), preferred_element_type=jnp.float32
     )
-    scaled_grad = normed_grad * gain_full
-    inner_mean = jnp.mean(scaled_grad * inputs_wide, axis=-1)
-    scale_col = inverse[:, None]
+    scaled_grad = normed_grad * gain_local
+    inner_part = jnp.sum(scaled_grad * x_wide, axis=-1)
+    inner_mean = jnp.sum(lax.all_gather(inner_part, "dp", axis=0), axis=0) / feature_count
     input_grad = (
-        scale_col * scaled_grad - inputs_wide * scale_col**3 * inner_mean[:, None]
+        scale_col * scaled_grad - x_wide * scale_col**3 * inner_mean[:, None]
     ).astype(jnp.bfloat16)
-    gain_term = jnp.sum(normed_grad * inputs_wide * scale_col, axis=0)
-    gain_grad = lax.psum(gain_term, "dp")
-    upstream = shifted(input_grad.reshape(micro_count, seq_len, feature_count), "pipe", -1)
+    gain_part = jnp.sum(normed_grad * x_wide * scale_col, axis=0)
+    gain_grad = lax.all_gather(gain_part, "dp", axis=0, tiled=True)
+
+    upstream = jnp.zeros((token_count, feature_count), jnp.bfloat16)
+    for k in range(replicas):
+        pairs = [
+            (s * replicas + d, (s - 1) * replicas + (d + k) % replicas)
+            for s in range(1, sections)
+            for d in range(replicas)
+        ]
+        dest = (me + k) % replicas
+        block = lax.dynamic_slice_in_dim(input_grad, dest * token_count, token_count, axis=0)
+        got = lax.ppermute(block, axes, pairs)
+        upstream = lax.dynamic_update_slice_in_dim(
+            upstream, got, ((me - k) % replicas) * width, axis=1
+        )
+    upstream = upstream.reshape(micro_count, seq_len, feature_count)
     return (upstream[None], weight_grad[None], gain_grad[None])
 
 

time: 502 us -> 382 us (0.76)
  blocking collectives: 191 us -> 39.4 us
  waiting for transfers between devices: 133 us -> 213 us
  local copies, waits for them, and re-layouts: 63.5 us -> 22 us
  other arithmetic: 25.2 us -> 18.5 us
    ppermute x1 -> x12, waiting for transfers between devices: 0.01 us -> 134 us  [the longest x8 93 us: local(): received.append(lax.ppermute((block, inv_src), axes, pairs))]
    all_gather x1 -> x0, waiting for transfers between devices: 76.3 us -> none  [local(): full_weight = lax.all_gather(local_weight, 'dp', axis=0, tiled=True)]
    all_to_all x1 -> x0, blocking collectives: 69.4 us -> none  [local(): lax.all_to_all(flat_stored, 'pipe', split_axis=1, concat_axis=0, tiled=True)]
    all_gather x1 -> x3, blocking collectives: 108 us -> 39.4 us  [the longest x1 28.4 us: local(): gain_grad = lax.all_gather(gain_part, 'dp', axis=0, tiled=True)]
    all_to_all x2 -> x0, waiting for transfers between devices: 55.9 us -> none  [the longest x1 55.9 us: local(): lax.all_to_all(blocks, 'pipe', split_axis=0, concat_axis=2, tiled=True)]
    reduce_scatter x0 -> x1, waiting for transfers between devices: none -> 49.6 us  [local(): projected = lax.psum_scatter(partial, 'dp', scatter_dimension=0, tiled=True)]
    all_gather x1, waiting for transfers between devices: 0.01 us -> 29.7 us  [local(): all_kv_grads = lax.all_gather(kv_grads, 'dp', axis=0, tiled=True)]
    ppermute x1 -> x12, starting transfers between devices: 11.4 us -> 29.1 us  [the longest x8 15.5 us: local(): received.append(lax.ppermute((block, inv_src), axes, pairs))]
  transfers between devices with their start and end apart: 5 -> 14, of which waited for: 2 -> 9; matrix products, arithmetic and copies ran while one was open for 26% -> 5% of each run, Pallas kernels for 0% -> 0%
where the time goes in v1:
time: 382 us; the launch traced here: 377 us
  waiting for transfers between devices  213 us (56%)
  matrix products  40.1 us (10%)
  blocking collectives  39.4 us (10%)
  starting transfers between devices  29.4 us (8%)
  local copies, waits for them, and re-layouts  22 us (6%)
  other arithmetic  18.5 us (5%)
  between operations  14.5 us (4%)
    ppermute x8, waiting for transfers between devices, local(): received.append(lax.ppermute((block, inv_src), axes, pairs))  93 us
    reduce_scatter x1, waiting for transfers between devices, local(): projected = lax.psum_scatter(partial, 'dp', scatter_dimension=0, tiled=True)  49.6 us
    ppermute x4, waiting for transfers between devices, local(): got = lax.ppermute(block, axes, pairs)  40.8 us
    all_gather x1, waiting for transfers between devices, local(): all_kv_grads = lax.all_gather(kv_grads, 'dp', axis=0, tiled=True)  29.7 us
    all_gather x1, blocking collectives, local(): gain_grad = lax.all_gather(gain_part, 'dp', axis=0, tiled=True)  28.4 us
    ppermute x8, starting transfers between devices, local(): received.append(lax.ppermute((block, inv_src), axes, pairs))  15.5 us
    ppermute x4, starting transfers between devices, local(): got = lax.ppermute(block, axes, pairs)  13.6 us
    dot_general x1, matrix products, local(): lax.dot_general(all_kv_grads, local_weight, (((1,), (1,)), ((), ())), pre...  11.8 us
  transfers between devices with their start and end apart: 14, of which 9 were waited for; matrix products, arithmetic and copies ran while one was open for 5% of the time, Pallas kernels for 0%

profile of v1, /device:TPU:66, one launch (start us, length us, event | category | flops | bytes accessed | tf_op | source)
XLA Modules:
  0.0 376.8 jit_solution(6536535668559132017)
XLA Ops:
  7.3 3.7 constant_dynamic-slice_fusion.7
  11.0 3.7 collective-permute-start.4
  15.5 3.5 collective-permute-start.6
  23.5 5.8 %all-gather = s32[4,1,2]{2,1,0:T(1,128)S(1)} all-gather(s32[1,1,2]{2,1,0:T(1,128)S(1)} %copy-done.4), channel_id=2, replica_groups=mesh['pipe'=32,'dp'=4] {'dp'}, dimensions={0}, use_global_device_ids=true | all-gather | bytes 40 | tf_op jit(solution)/shard_map/all_gather | solution.py:78
  30.3 78.1 %collective-permute-done = f32[256]{0:T(256)S(1)} collective-permute-done((f32[256]{0:T(256)S(1)}, f32[256]{0:T(256)S(1)}, u32[]{:S(2)}, u32[]{:S(2)}) %collective-permute-start) | collective-permute-done | bytes 1056 | tf_op jit(solution)/shard_map/ppermute | solution.py:76
  109.3 5.1 %collective-permute-done.1 = f32[256]{0:T(256)S(1)} collective-permute-done((f32[256]{0:T(256)S(1)}, f32[256]{0:T(256)S(1)}, u32[]{:S(2)}, u32[]{:S(2)}) %collective-permute-start.1) | collective-permute-done | bytes 1056 | tf_op jit(solution)/shard_map/ppermute | solution.py:76
  117.1 3.9 %collective-permute-done.2 = f32[256]{0:T(256)S(1)} collective-permute-done((f32[256]{0:T(256)S(1)}, f32[256]{0:T(256)S(1)}, u32[]{:S(2)}, u32[]{:S(2)}) %collective-permute-start.2) | collective-permute-done | bytes 1056 | tf_op jit(solution)/shard_map/ppermute | solution.py:76
  121.5 5.8 %collective-permute-done.3 = f32[256]{0:T(256)S(1)} collective-permute-done((f32[256]{0:T(256)S(1)}, f32[256]{0:T(256)S(1)}, u32[]{:S(2)}, u32[]{:S(2)}) %collective-permute-start.3) | collective-permute-done | bytes 1056 | tf_op jit(solution)/shard_map/ppermute | solution.py:76
  128.0 3.8 %pad_maximum_fusion = bf16[4,256,2048]{2,1,0:T(8,128)(2,1)} fusion(bf16[1,256,2048]{2,1,0:T(8,128)(2,1)} %bitcast.14, bf16[1,256,2048]{2,1,0:T(8,128)(2,1)} %bitcast.13, bf16[1,256,2048]{2,1,0:T(8,128)(2,1)} %bitcast.12, bf16[1,256,2048]{2,1,0:T(8,128)(2,1)} %bitcast.11), kind=kLoop, calls=%fused_computation.19 | loop fusion | flops 6291456 | bytes 8388608 | tf_op jit(solution)/shard_map/stack | solution.py:82
  131.8 5.0 %gather_fusion.1 = bf16[8,128,2048]{2,1,0:T(8,128)(2,1)} fusion(bf16[8,128,2048]{2,1,0:T(8,128)(2,1)} %bitcast.131, s32[1024]{0:T(1024)S(1)} %pad_clamp_fusion), kind=kCustom, calls=%fused_computation.1 | custom fusion | bytes 8388640 | tf_op jit(solution)/shard_map/jit(_take)/gather | solution.py:84
  136.8 3.8 multiply_convert_fusion
  140.6 6.0 %fusion.17 = f32[1024,1024]{1,0:T(8,128)} fusion(bf16[1024,2048]{1,0:T(8,128)(2,1)S(1)} %bitcast.137, bf16[1,2048,1024]{2,1,0:T(8,128)(2,1)S(1)} %copy-done.5), kind=kOutput, calls=%fused_computation.29 | convolution fusion | flops 4294967296 | bytes 12582912 | tf_op jit(solution)/shard_map/dot_general | solution.py:93
  152.5 49.6 %reduce-scatter.2.cloned.1.call-done = f32[256,1024]{1,0:T(8,128)} async-done(((f32[1024,1024]{1,0:T(8,128)}), f32[256,1024]{1,0:T(8,128)}) %reduce-scatter.2.cloned.1.call-update) | async-done | bytes 1048592 | tf_op jit(solution)/shard_map/reduce_scatter | solution.py:94
  210.3 7.5 %fusion.58 = bf16[2,128,4,128]{3,1,2,0:T(8,128)(2,1)S(1)} fusion(bf16[2,128,4,8,128]{4,3,2,1,0:T(8,128)(2,1)S(1)} %bitcast.133, f32[2,4,128,128,8]{3,2,4,1,0:T(8,128)} %fusion.32, f32[2,4,8,128,128]{3,4,2,1,0:T(8,128)} %copy-done.6, f32[2,4,8,128]{3,2,1,0:T(8,128)S(1)} %get-tuple-element.18), kind=kOutput, calls=%fused_computation.55 | convolution fusion | flops 275914880 | bytes 10780672 | tf_op jit(solution)/shard_map/bhgqk,bqhgd->bkhd/dot_general | solution.py:45
  219.4 29.7 %all-gather.4.cloned.1.call-done = bf16[1024,1024]{1,0:T(8,128)(2,1)} async-done(((bf16[256,1024]{1,0:T(8,128)(2,1)}), bf16[1024,1024]{1,0:T(8,128)(2,1)}) %all-gather.4.cloned.1.call-update) | async-done | bytes 2097168 | tf_op jit(solution)/shard_map/all_gather | solution.py:105
  249.1 11.8 %fusion.9 = (f32[2048]{0:T(1024)S(1)}, f32[1024]{0:T(1024)S(1)}, bf16[1024,2048]{1,0:T(8,128)(2,1)}, f32[1024,2048]{1,0:T(8,128)}) fusion(f32[1024]{0:T(1024)S(1)} %get-tuple-element.6, f32[2048]{0:T(1024)S(1)} %bitcast.147, bf16[8,128,2048]{2,1,0:T(8,128)(2,1)} %gather_fusion.1, pred[1024]{0:T(1024)(128)(4,1)S(1)} %broadcast_bitcast_fusion, ...), kind=kOutput, calls=%fused_computation.15 | convolution fusion | flops 4311741440 | bytes 23094272 | tf_op jit(solution)/shard_map/dot_general | solution.py:109
  260.9 5.2 %all-gather.1 = f32[4096]{0:T(1024)S(1)} all-gather(f32[1024]{0:T(1024)S(1)} %get-tuple-element.4), channel_id=3, replica_groups=mesh['pipe'=32,'dp'=4] {'dp'}, dimensions={0}, use_global_device_ids=true | all-gather | bytes 20480 | tf_op jit(solution)/shard_map/all_gather | solution.py:114
  266.1 5.6 %fusion.4 = bf16[1024,2048]{1,0:T(8,128)(2,1)S(1)} fusion(bf16[1024,2048]{1,0:T(8,128)(2,1)} %get-tuple-element.7, f32[1024,2048]{1,0:T(8,128)} %get-tuple-element.20, f32[1024]{0:T(1024)S(1)} %broadcast_multiply_fusion, f32[1024]{0:T(1024)S(1)} %get-tuple-element.5, f32[2048]{0:T(1024)S(1)} %bitcast.148, f32[1024]{0:T(1024)S(1)} %get-tuple-element.6), kind=kLoop, calls=%fused_computation.10 | loop fusion | flops 14680064 | bytes 16797696 | tf_op jit(solution)/shard_map/convert_element_type | solution.py:117
  273.2 4.5 %collective-permute-start.8 = (bf16[256,2048]{1,0:T(8,128)(2,1)}, bf16[256,2048]{1,0:T(8,128)(2,1)}, u32[]{:S(2)}, u32[]{:S(2)}) collective-permute-start(bf16[256,2048]{1,0:T(8,128)(2,1)} %get-tuple-element.11), channel_id=1, source_target_pairs={{4,0},{5,1},{6,2},{7,3},{8,4},{9,5},{10,6},{11,7},{12,8},{13,9},{1... | collective-permute-start | bytes 3145736 | tf_op jit(solution)/shard_map/ppermute | solution.py:130
  280.1 3.9 %collective-permute-start.10 = (bf16[256,2048]{1,0:T(8,128)(2,1)S(1)}, bf16[256,2048]{1,0:T(8,128)(2,1)S(1)}, u32[]{:S(2)}, u32[]{:S(2)}) collective-permute-start(bf16[256,2048]{1,0:T(8,128)(2,1)S(1)} %get-tuple-element.9), channel_id=1, source_target_pairs={{4,2},{5,3},{6,0},{7,1},{8,6},{9,7},{10,4},{11,5},{12,10},{13,11},... | collective-permute-start | bytes 3145736 | tf_op jit(solution)/shard_map/ppermute | solution.py:130
  286.8 9.8 %convert_bitcast_fusion = bf16[1,2048,1024]{2,1,0:T(8,128)(2,1)} fusion(bf16[1024,1024]{1,0:T(8,128)(2,1)} %all-gather.4.cloned.1.call-done, bf16[1024,2048]{1,0:T(8,128)(2,1)} %get-tuple-element.7, f32[2048]{0:T(1024)S(1)} %bitcast.149, f32[1024]{0:T(1024)S(1)} %get-tuple-element.6), kind=kOutput, calls=%fused_computation.31 | convolution fusion | flops 4305453056 | bytes 10498048 | tf_op jit(solution)/shard_map/dot_general | solution.py:106
  296.7 28.4 %all_gather.19 = f32[8192]{0:T(1024)S(1)} all-gather(f32[2048]{0:T(1024)S(1)} %get-tuple-element.3), channel_id=1, replica_groups=mesh['pipe'=32,'dp'=4] {'dp'}, dimensions={0}, use_global_device_ids=true | all-gather | bytes 40960 | tf_op jit(solution)/shard_map/all_gather | solution.py:119
  326.8 20.2 %collective-permute-done.9 = bf16[256,2048]{1,0:T(8,128)(2,1)S(1)} collective-permute-done((bf16[256,2048]{1,0:T(8,128)(2,1)S(1)}, bf16[256,2048]{1,0:T(8,128)(2,1)S(1)}, u32[]{:S(2)}, u32[]{:S(2)}) %collective-permute-start.9) | collective-permute-done | bytes 1048608 | tf_op jit(solution)/shard_map/ppermute | solution.py:130
  347.3 20.6 %collective-permute-done.11 = bf16[256,2048]{1,0:T(8,128)(2,1)S(1)} collective-permute-done((bf16[256,2048]{1,0:T(8,128)(2,1)S(1)}, bf16[256,2048]{1,0:T(8,128)(2,1)S(1)}, u32[]{:S(2)}, u32[]{:S(2)}) %collective-permute-start.11) | collective-permute-done | bytes 1048608 | tf_op jit(solution)/shard_map/ppermute | solution.py:130
  (76 shorter events, 37.3 us)
Async XLA Ops:
  7.2 194.9 %reduce-scatter.2.cloned.1.call-start = ((), (), s32[]{:S(2)}) async-start(), calls=%async_computation.1 | async-start | bytes 5242880 | tf_op jit(solution)/shard_map/reduce_scatter | solution.py:94
  7.3 14.3 %copy-start = (bf16[1,2,128,8192]{3,2,1,0:T(8,128)(2,1)S(1)}, bf16[1,2,128,8192]{3,2,1,0:T(8,128)(2,1)}, u32[]{:S(2)}) copy-start(bf16[1,2,128,8192]{3,2,1,0:T(8,128)(2,1)} %param.7) | copy-start | bytes 12582916
  11.0 12.5 %copy-start.4 = (s32[1,1,2]{2,1,0:T(1,128)S(1)}, s32[1,1,2]{2,1,0:T(1,128)}, u32[]{:S(2)}) copy-start(s32[1,1,2]{2,1,0:T(1,128)} %param.8) | copy-start | bytes 28
  11.0 117.0 %collective-permute-start.4 = (bf16[256,2048]{1,0:T(8,128)(2,1)}, bf16[256,2048]{1,0:T(8,128)(2,1)}, u32[]{:S(2)}, u32[]{:S(2)}) collective-permute-start(bf16[256,2048]{1,0:T(8,128)(2,1)} %get-tuple-element.12), channel_id=1, source_target_pairs={{0,124},{1,125},{2,126},{3,127},{4,120},{5,121},{6,122},{7,123},{8... | collective-permute-start | bytes 3145736 | tf_op jit(solution)/shard_map/ppermute | solution.py:76
  14.7 113.3 %collective-permute-start.5 = (bf16[256,2048]{1,0:T(8,128)(2,1)S(1)}, bf16[256,2048]{1,0:T(8,128)(2,1)}, u32[]{:S(2)}, u32[]{:S(2)}) collective-permute-start(bf16[256,2048]{1,0:T(8,128)(2,1)S(1)} %get-tuple-element.15), channel_id=1, source_target_pairs={{0,125},{1,126},{2,127},{3,124},{4,121},{5,122},{6,123},{7,120},{8... | collective-permute-start | bytes 3145736 | tf_op jit(solution)/shard_map/ppermute | solution.py:76
  15.5 112.5 %collective-permute-start.6 = (bf16[256,2048]{1,0:T(8,128)(2,1)S(1)}, bf16[256,2048]{1,0:T(8,128)(2,1)}, u32[]{:S(2)}, u32[]{:S(2)}) collective-permute-start(bf16[256,2048]{1,0:T(8,128)(2,1)S(1)} %get-tuple-element.14), channel_id=1, source_target_pairs={{0,126},{1,127},{2,124},{3,125},{4,122},{5,123},{6,120},{7,121},{8... | collective-permute-start | bytes 3145736 | tf_op jit(solution)/shard_map/ppermute | solution.py:76
  19.0 109.0 %collective-permute-start.7 = (bf16[256,2048]{1,0:T(8,128)(2,1)S(1)}, bf16[256,2048]{1,0:T(8,128)(2,1)}, u32[]{:S(2)}, u32[]{:S(2)}) collective-permute-start(bf16[256,2048]{1,0:T(8,128)(2,1)S(1)} %get-tuple-element.13), channel_id=1, source_target_pairs={{0,127},{1,124},{2,125},{3,126},{4,123},{5,120},{6,121},{7,122},{8... | collective-permute-start | bytes 3145736 | tf_op jit(solution)/shard_map/ppermute | solution.py:76
  22.5 86.0 %collective-permute-start = (f32[256]{0:T(256)S(1)}, f32[256]{0:T(256)S(1)}, u32[]{:S(2)}, u32[]{:S(2)}) collective-permute-start(f32[256]{0:T(256)S(1)} %rsqrt_bitcast_fusion), channel_id=1, source_target_pairs={{0,124},{1,125},{2,126},{3,127},{4,120},{5,121},{6,122},{7,123},{8... | collective-permute-start | bytes 3080 | tf_op jit(solution)/shard_map/ppermute | solution.py:76
  108.4 6.0 %collective-permute-start.1 = (f32[256]{0:T(256)S(1)}, f32[256]{0:T(256)S(1)}, u32[]{:S(2)}, u32[]{:S(2)}) collective-permute-start(f32[256]{0:T(256)S(1)} %rsqrt_bitcast_fusion), channel_id=1, source_target_pairs={{0,125},{1,126},{2,127},{3,124},{4,121},{5,122},{6,123},{7,120},{8... | collective-permute-start | bytes 3080 | tf_op jit(solution)/shard_map/ppermute | solution.py:76
  114.4 6.6 %collective-permute-start.2 = (f32[256]{0:T(256)S(1)}, f32[256]{0:T(256)S(1)}, u32[]{:S(2)}, u32[]{:S(2)}) collective-permute-start(f32[256]{0:T(256)S(1)} %rsqrt_bitcast_fusion), channel_id=1, source_target_pairs={{0,126},{1,127},{2,124},{3,125},{4,122},{5,123},{6,120},{7,121},{8... | collective-permute-start | bytes 3080 | tf_op jit(solution)/shard_map/ppermute | solution.py:76
  121.0 6.3 %collective-permute-start.3 = (f32[256]{0:T(256)S(1)}, f32[256]{0:T(256)S(1)}, u32[]{:S(2)}, u32[]{:S(2)}) collective-permute-start(f32[256]{0:T(256)S(1)} %rsqrt_bitcast_fusion), channel_id=1, source_target_pairs={{0,127},{1,124},{2,125},{3,126},{4,123},{5,120},{6,121},{7,122},{8... | collective-permute-start | bytes 3080 | tf_op jit(solution)/shard_map/ppermute | solution.py:76
  136.8 3.8 %copy-start.5 = (bf16[1,2048,1024]{2,1,0:T(8,128)(2,1)S(1)}, bf16[1,2048,1024]{2,1,0:T(8,128)(2,1)}, u32[]{:S(2)}) copy-start(bf16[1,2048,1024]{2,1,0:T(8,128)(2,1)} %param.13) | copy-start | bytes 12582916
  146.6 102.4 %all-gather.4.cloned.1.call-start = ((), (), s32[]{:S(2)}) async-start(), calls=%async_computation.2 | async-start | bytes 2621440 | tf_op jit(solution)/shard_map/all_gather | solution.py:105
  146.9 5.5 %copy-start.3 = (s32[1,2,128]{2,1,0:T(2,128)S(1)}, s32[1,2,128]{2,1,0:T(2,128)}, u32[]{:S(2)}) copy-start(s32[1,2,128]{2,1,0:T(2,128)} %param.9) | copy-start | bytes 3076
  204.7 1.6 copy-start.1
  205.9 3.4 copy-start.6
  273.2 51.9 %collective-permute-start.8 = (bf16[256,2048]{1,0:T(8,128)(2,1)}, bf16[256,2048]{1,0:T(8,128)(2,1)}, u32[]{:S(2)}, u32[]{:S(2)}) collective-permute-start(bf16[256,2048]{1,0:T(8,128)(2,1)} %get-tuple-element.11), channel_id=1, source_target_pairs={{4,0},{5,1},{6,2},{7,3},{8,4},{9,5},{10,6},{11,7},{12,8},{13,9},{1... | collective-permute-start | bytes 3145736 | tf_op jit(solution)/shard_map/ppermute | solution.py:130
  277.7 69.3 %collective-permute-start.9 = (bf16[256,2048]{1,0:T(8,128)(2,1)S(1)}, bf16[256,2048]{1,0:T(8,128)(2,1)S(1)}, u32[]{:S(2)}, u32[]{:S(2)}) collective-permute-start(bf16[256,2048]{1,0:T(8,128)(2,1)S(1)} %get-tuple-element.10), channel_id=1, source_target_pairs={{4,1},{5,2},{6,3},{7,0},{8,5},{9,6},{10,7},{11,4},{12,9},{13,10},{... | collective-permute-start | bytes 3145736 | tf_op jit(solution)/shard_map/ppermute | solution.py:130
  280.1 67.1 %collective-permute-start.10 = (bf16[256,2048]{1,0:T(8,128)(2,1)S(1)}, bf16[256,2048]{1,0:T(8,128)(2,1)S(1)}, u32[]{:S(2)}, u32[]{:S(2)}) collective-permute-start(bf16[256,2048]{1,0:T(8,128)(2,1)S(1)} %get-tuple-element.9), channel_id=1, source_target_pairs={{4,2},{5,3},{6,0},{7,1},{8,6},{9,7},{10,4},{11,5},{12,10},{13,11},... | collective-permute-start | bytes 3145736 | tf_op jit(solution)/shard_map/ppermute | solution.py:130
  284.1 83.8 %collective-permute-start.11 = (bf16[256,2048]{1,0:T(8,128)(2,1)S(1)}, bf16[256,2048]{1,0:T(8,128)(2,1)S(1)}, u32[]{:S(2)}, u32[]{:S(2)}) collective-permute-start(bf16[256,2048]{1,0:T(8,128)(2,1)S(1)} %get-tuple-element.8), channel_id=1, source_target_pairs={{4,3},{5,0},{6,1},{7,2},{8,7},{9,4},{10,5},{11,6},{12,11},{13,8},{... | collective-permute-start | bytes 3145736 | tf_op jit(solution)/shard_map/ppermute | solution.py:130
  368.0 2.0 copy-start.2
Sparse Core Ops, SparseCore 0:
  146.8 55.2 reduce-scatter.1
  219.3 29.6 all-gather.3
